TPU v7x, 32 devices: a whole 2x2x4 slice. The times are simulated.
32 devices in a mesh: dp: 8 (over z, y), tensor: 4 (over x, core).
Axes of the slice: x: 2, y: 2, z: 4, core: 2. Of those that a mesh axis runs over, the one named last changes fastest.
Arguments:
- hidden: bfloat16 [2048, 1024], P('dp'), may hold values from -6 to 6
- lengths: int32 [8, 16], P('dp'), may hold values from 1 to 64, 256 in all within a row
- w_qkv: bfloat16 [3, 1024, 1024], P(None, None, 'tensor')
- b_qkv: float32 [3, 1024], P(None, 'tensor'), may hold values from -3 to 3
- w_output: bfloat16 [1024, 1024], P('tensor'), may hold values from -0.1875 to 0.1875
- b_output: float32 [1024], replicated, may hold values from -3 to 3
- first_gain: float32 [1024], replicated, may hold values from 0.25 to 1.75
- first_shift: float32 [1024], replicated, may hold values from -3 to 3
- w_up: bfloat16 [1024, 4096], P(None, 'tensor'), may hold values from -0.1875 to 0.1875
- b_up: float32 [4096], P('tensor'), may hold values from -3 to 3
- w_down: bfloat16 [4096, 1024], P('tensor'), may hold values from -0.09375 to 0.09375
- b_down: float32 [1024], replicated, may hold values from -3 to 3
- second_gain: float32 [1024], replicated, may hold values from 0.25 to 1.75
- second_shift: float32 [1024], replicated, may hold values from -3 to 3
- index: bfloat16 [16384, 1024], P('dp', 'tensor'), may hold values from -6 to 6
- candidates: int32 [128, 64], replicated, may hold values from 0 to 16383, as said below
Outputs:
- states: bfloat16 [2048, 1024], P('dp')
- scores: float32 [128, 64], P('dp')
Inputs may be any that keep to these rules, and one draw needn't show every extreme that they name: `candidates`: each index of dp holds exactly 1024 of the 8192 named rows, counted with repetition.
All inputs are finite; a program needn't handle non-finite values.
Results may differ from a plain program's by a relative error of at most 0.014.
Values may be sent and summed in bfloat16 or wider, within the bound.
No kernel may reach another device: no remote copies, remote signals or barrier semaphores. Data moves between devices by JAX's collectives and lax.ppermute only.
A program may use at most 64 MiB of HBM per device.

v0:
```python
import math
import jax
import jax.numpy as jnp
from jax import lax
from jax.sharding import PartitionSpec as P

HEAD = 64


def layer_norm(values, gain, shift):
    centre = jnp.mean(values, axis=-1, keepdims=True)
    centred = values - centre
    spread = jnp.mean(centred * centred, axis=-1, keepdims=True)
    return centred * lax.rsqrt(spread + 1e-05) * gain + shift


def segment_of(pack_lengths, count):
    ends = jnp.cumsum(pack_lengths)
    position = jnp.arange(count, dtype=jnp.int32)
    return jnp.sum((position[:, None] >= ends[None, :]).astype(jnp.int32), axis=1)


def settle_attention(partial_value, residual, bias, gain, shift):
    total = lax.psum(partial_value.astype(jnp.bfloat16), "tensor").astype(jnp.float32)
    return layer_norm(total + bias + residual.astype(jnp.float32), gain, shift).astype(jnp.bfloat16)


def settle_forward(partial_value, residual, bias, gain, shift):
    total = lax.psum(partial_value.astype(jnp.bfloat16), "tensor").astype(jnp.float32)
    return layer_norm(total + bias + residual.astype(jnp.float32), gain, shift).astype(jnp.bfloat16)


def body(
    hidden,
    lengths,
    w_qkv,
    b_qkv,
    w_output,
    b_output,
    first_gain,
    first_shift,
    w_up,
    b_up,
    w_down,
    b_down,
    second_gain,
    second_shift,
    index,
    candidates,
):
    tokens_here = hidden.shape[0]
    local_width = w_qkv.shape[2]
    local_heads = local_width // HEAD
    projected = [
        jnp.dot(hidden, w_qkv[j], preferred_element_type=jnp.float32) + b_qkv[j] for j in range(3)
    ]
    queries = (projected[0] * 0.125).astype(jnp.bfloat16).reshape(tokens_here, local_heads, HEAD)
    keys = projected[1].astype(jnp.bfloat16).reshape(tokens_here, local_heads, HEAD)
    values = projected[2].astype(jnp.bfloat16).reshape(tokens_here, local_heads, HEAD)
    segment = segment_of(lengths[0], tokens_here)
    same = segment[:, None] == segment[None, :]
    logits = jnp.einsum("thd,shd->hts", queries, keys, preferred_element_type=jnp.float32)
    logits = jnp.where(same[None], logits, -1e30)
    top = jnp.max(logits, axis=-1, keepdims=True)
    expo = jnp.exp(logits - top)
    weights = (expo / jnp.sum(expo, axis=-1, keepdims=True)).astype(jnp.bfloat16)
    context = jnp.einsum("hts,shd->thd", weights, values, preferred_element_type=jnp.float32)
    context = context.astype(jnp.bfloat16).reshape(tokens_here, local_width)
    partial_value = jnp.dot(context, w_output, preferred_element_type=jnp.float32)
    attended = settle_attention(partial_value, hidden, b_output, first_gain, first_shift)
    activated = jax.nn.gelu(
        jnp.dot(attended, w_up, preferred_element_type=jnp.float32) + b_up, approximate=False
    ).astype(jnp.bfloat16)
    partial_value = jnp.dot(activated, w_down, preferred_element_type=jnp.float32)
    states = settle_forward(partial_value, attended, b_down, second_gain, second_shift)
    texts_here = lengths.shape[1]
    member = (segment[None, :] == jnp.arange(texts_here, dtype=jnp.int32)[:, None]).astype(
        jnp.bfloat16
    )
    pooled = (
        jnp.dot(member, states, preferred_element_type=jnp.float32)
        / lengths[0].astype(jnp.float32)[:, None]
    )
    unit = pooled * lax.rsqrt(jnp.sum(pooled * pooled, axis=-1, keepdims=True) + 1e-06)
    quarter = index.shape[1]
    unit_quarter = lax.dynamic_slice_in_dim(
        unit, lax.axis_index("tensor") * quarter, quarter, 1
    ).astype(jnp.bfloat16)
    row_base = lax.axis_index("dp") * index.shape[0]
    gathered = lax.all_gather(unit_quarter, "dp", axis=0, tiled=True)
    all_texts = candidates.shape[0]
    cand_count = candidates.shape[1]
    shard_rows = index.shape[0]
    block_rows = math.gcd(all_texts, 128)
    block_count = all_texts // block_rows
    local_rows = candidates - row_base
    row_ids = jnp.arange(shard_rows, dtype=jnp.int32)

    def score_block(packed):
        query_block, wanted = packed
        tile = lax.dot_general(
            query_block, index, (((1,), (1,)), ((), ())), preferred_element_type=jnp.float32
        )
        chosen = wanted[:, :, None] == row_ids[None, None, :]
        return jnp.sum(jnp.where(chosen, tile[:, None, :], 0.0), axis=2)

    partial_scores = lax.map(
        score_block,
        (
            gathered.reshape(block_count, block_rows, quarter),
            local_rows.reshape(block_count, block_rows, cand_count),
        ),
    )
    partial_scores = partial_scores.reshape(all_texts, cand_count)
    slice_scores = lax.psum_scatter(
        partial_scores, ("dp", "tensor"), scatter_dimension=0, tiled=True
    )
    scores = lax.all_gather(slice_scores, "tensor", axis=0, tiled=True)
    return (states, scores)


def solution(mesh):
    placed = (
        P("dp", None),
        P("dp", None),
        P(None, None, "tensor"),
        P(None, "tensor"),
        P("tensor", None),
        P(),
        P(),
        P(),
        P(None, "tensor"),
        P("tensor"),
        P("tensor", None),
        P(),
        P(),
        P(),
        P("dp", "tensor"),
        P(),
    )
    return jax.shard_map(
        body, mesh=mesh, in_specs=placed, out_specs=(P("dp", None), P("dp", None)), check_vma=False
    )
```

profile of v0, /device:TPU:15, one launch (start us, length us, event | category | flops | bytes accessed | tf_op | source)
XLA Modules:
  0.0 194.1 jit_solution(16302811454098410085)
XLA Ops:
  7.2 0.0 all-reduce.4.cloned.1.call-start
  7.2 0.9 fusion.90
  8.1 1.6 fusion.6
  9.7 1.6 fusion.5
  11.3 0.1 copy.27
  11.4 0.1 reduce
  11.6 0.1 convert_reduce_fusion
  11.6 0.1 broadcast_compare_fusion
  11.8 1.3 convolution_select_fusion
  13.1 0.5 fusion.91
  13.6 1.4 fusion.4
  15.1 2.0 %convolution_convert_fusion.2 = bf16[4,64,256]{2,1,0:T(8,128)(2,1)S(1)} fusion(bf16[256,4,64]{0,2,1:T(8,128)(2,1)S(1)} %bitcast.51, f32[4,256]{1,0:T(4,128)S(1)} %fusion.91, f32[4,256,256]{1,2,0:T(8,128)} %convolution_select_fusion), kind=kOutput, calls=%fused_computation.14 | convolution fusion | flops 34407680 | bytes 1314816 | tf_op jit(solution)/shard_map/hts,shd->thd/dot_general | solution.py:67
  17.1 1.1 convolution_convert_fusion
  18.2 0.0 all-reduce.6.cloned.1.call-start
  18.3 32.6 %all-reduce.4.cloned.1.call-done = bf16[256,1024]{1,0:T(8,128)(2,1)} async-done(((bf16[256,1024]{1,0:T(8,128)(2,1)}), bf16[256,1024]{1,0:T(8,128)(2,1)}) %all-reduce.4.cloned.1.call-update) | async-done | bytes 524304 | tf_op jit(solution)/shard_map/psum | solution.py:24
  50.8 1.4 fusion.17
  52.2 1.4 multiply_reduce_fusion.1
  53.6 0.3 add_convert_fusion.1
  54.0 5.9 %convolution_convert_fusion.1 = bf16[256,1024]{1,0:T(8,128)(2,1)} fusion(bf16[1024,1024]{1,0:T(8,128)(2,1)S(1)} %copy-done, bf16[256,1024]{1,0:T(8,128)(2,1)S(1)} %add_convert_fusion.1, bf16[1024,1024]{1,0:T(8,128)(2,1)} %param.24, f32[1024]{0:T(1024)S(1)} %copy-done.15), kind=kOutput, calls=%fused_computation.9 | convolution fusion | flops 1091305472 | bytes 5246976 | tf_op jit(solution)/shard_map/dot_general | solution.py:74
  59.9 0.1 copy.29
  60.1 33.2 %all-reduce.6.cloned.1.call-done = bf16[256,1024]{1,0:T(8,128)(2,1)} async-done(((bf16[256,1024]{1,0:T(8,128)(2,1)}), bf16[256,1024]{1,0:T(8,128)(2,1)}) %all-reduce.6.cloned.1.call-update) | async-done | bytes 524304 | tf_op jit(solution)/shard_map/psum | solution.py:29
  93.3 1.4 fusion.18
  94.7 1.4 multiply_reduce_fusion
  96.1 0.3 add_convert_fusion
  96.4 0.3 multiply_reduce_fusion.2
  96.7 0.1 fusion.56
  96.8 21.9 %all_gather.6 = bf16[128,256]{1,0:T(8,128)(2,1)S(1)} all-gather(bf16[16,256]{1,0:T(8,128)(2,1)S(1)} %fusion.56), channel_id=1, replica_groups=mesh['dp'=8,'tensor'=4] {'dp'}, dimensions={0}, use_global_device_ids=true | all-gather | bytes 73728 | tf_op jit(solution)/shard_map/all_gather | solution.py:90
  118.7 0.5 fusion.92
  119.2 10.9 %select_reduce_fusion = f32[128,64]{1,0:T(8,128)S(1)} fusion(f32[128,2048]{1,0:T(8,128)S(1)} %fusion.92, s32[128,64]{1,0:T(8,128)S(1)} %copy.29), kind=kLoop, calls=%fused_computation.1 | loop fusion | flops 50323456 | bytes 1114112 | tf_op jit(solution)/shard_map/while/body/eval_jaxpr/reduce_sum | solution.py:105
  130.1 49.1 %all-reduce = f32[128,64]{1,0:T(8,128)S(1)} all-reduce(f32[128,64]{1,0:T(8,128)S(1)} %select_reduce_fusion), channel_id=2, replica_groups=mesh['dp'=8,'tensor'=4] {'dp','tensor'}, use_global_device_ids=true, to_apply=%region_12.13.clone | all-reduce | flops 8192 | bytes 65536
  179.2 7.4 %all-gather = f32[4,4,64]{2,1,0:T(4,128)S(1)} all-gather(f32[1,4,64]{2,1,0:T(4,128)S(1)} %dynamic-slice_bitcast_fusion), channel_id=1, replica_groups=mesh['dp'=8,'tensor'=4] {'tensor'}, dimensions={0}, use_global_device_ids=true | all-gather | bytes 5120 | tf_op jit(solution)/shard_map/all_gather | solution.py:118
  186.6 0.6 copy.34
  (43 shorter events, 0.2 us)
Async XLA Ops:
  7.2 46.8 %copy-start = (bf16[1024,1024]{1,0:T(8,128)(2,1)S(1)}, bf16[1024,1024]{1,0:T(8,128)(2,1)}, u32[]{:S(2)}) copy-start(bf16[1024,1024]{1,0:T(8,128)(2,1)} %param.26) | copy-start | bytes 6291460
  7.2 4.1 %copy-start.14 = (s32[1,16]{1,0:T(1,128)S(1)}, s32[1,16]{1,0:T(1,128)}, u32[]{:S(2)}) copy-start(s32[1,16]{1,0:T(1,128)} %param.17) | copy-start | bytes 196
  7.2 43.6 %all-reduce.4.cloned.1.call-start = ((), (), s32[]{:S(2)}) async-start(), calls=%async_computation | async-start | bytes 1048576 | tf_op jit(solution)/shard_map/psum | solution.py:24
  9.7 4.0 %copy-start.1 = (bf16[256,1024]{1,0:T(8,128)(2,1)S(1)}, bf16[256,1024]{1,0:T(8,128)(2,1)}, u32[]{:S(2)}) copy-start(bf16[256,1024]{1,0:T(8,128)(2,1)} %param.16) | copy-start | bytes 1572868
  15.0 2.0 %copy-start.6 = (bf16[256,1024]{1,0:T(8,128)(2,1)S(1)}, bf16[256,1024]{1,0:T(8,128)(2,1)}, u32[]{:S(2)}) copy-start(bf16[256,1024]{1,0:T(8,128)(2,1)} %param.20) | copy-start | bytes 1572868
  15.0 35.8 %copy-start.7 = (f32[1024]{0:T(1024)S(1)}, f32[1024]{0:T(1024)}, u32[]{:S(2)}) copy-start(f32[1024]{0:T(1024)} %param.21) | copy-start | bytes 12292
  17.0 36.6 %copy-start.10 = (f32[1024]{0:T(1024)S(1)}, f32[1024]{0:T(1024)}, u32[]{:S(2)}) copy-start(f32[1024]{0:T(1024)} %param.23) | copy-start | bytes 12292
  17.0 36.5 %copy-start.11 = (f32[1024]{0:T(1024)S(1)}, f32[1024]{0:T(1024)}, u32[]{:S(2)}) copy-start(f32[1024]{0:T(1024)} %param.22) | copy-start | bytes 12292
  18.2 35.8 %copy-start.15 = (f32[1024]{0:T(1024)S(1)}, f32[1024]{0:T(1024)}, u32[]{:S(2)}) copy-start(f32[1024]{0:T(1024)} %param.25) | copy-start | bytes 12292
  18.2 75.1 %all-reduce.6.cloned.1.call-start = ((), (), s32[]{:S(2)}) async-start(), calls=%async_computation.1 | async-start | bytes 1048576 | tf_op jit(solution)/shard_map/psum | solution.py:29
  50.8 2.8 %copy-start.3 = (bf16[256,1024]{1,0:T(8,128)(2,1)S(1)}, bf16[256,1024]{1,0:T(8,128)(2,1)}, u32[]{:S(2)}) copy-start(bf16[256,1024]{1,0:T(8,128)(2,1)} %all-reduce.4.cloned.1.call-done) | copy-start | bytes 1572868
  53.9 6.0 %copy-start.9 = (s32[128,64]{0,1:T(8,128)S(1)}, s32[128,64]{0,1:T(8,128)}, u32[]{:S(2)}) copy-start(s32[128,64]{0,1:T(8,128)} %param.31) | copy-start | bytes 98308
  54.0 39.3 %copy-start.8 = (f32[1024]{0:T(1024)S(1)}, f32[1024]{0:T(1024)}, u32[]{:S(2)}) copy-start(f32[1024]{0:T(1024)} %param.27) | copy-start | bytes 12292
  59.9 36.2 %copy-start.12 = (f32[1024]{0:T(1024)S(1)}, f32[1024]{0:T(1024)}, u32[]{:S(2)}) copy-start(f32[1024]{0:T(1024)} %param.29) | copy-start | bytes 12292
  59.9 36.2 %copy-start.13 = (f32[1024]{0:T(1024)S(1)}, f32[1024]{0:T(1024)}, u32[]{:S(2)}) copy-start(f32[1024]{0:T(1024)} %param.28) | copy-start | bytes 12292
  93.3 2.8 %copy-start.2 = (bf16[256,1024]{1,0:T(8,128)(2,1)S(1)}, bf16[256,1024]{1,0:T(8,128)(2,1)}, u32[]{:S(2)}) copy-start(bf16[256,1024]{1,0:T(8,128)(2,1)} %all-reduce.6.cloned.1.call-done) | copy-start | bytes 1572868
  93.3 25.4 %copy-start.5 = (bf16[2048,256]{1,0:T(8,128)(2,1)S(1)}, bf16[2048,256]{1,0:T(8,128)(2,1)}, u32[]{:S(2)}) copy-start(bf16[2048,256]{1,0:T(8,128)(2,1)} %param.30) | copy-start | bytes 3145732
  96.4 90.8 %copy-start.4 = (bf16[256,1024]{1,0:T(8,128)(2,1)}, bf16[256,1024]{1,0:T(8,128)(2,1)S(1)}, u32[]{:S(2)}) copy-start(bf16[256,1024]{1,0:T(8,128)(2,1)S(1)} %add_convert_fusion) | copy-start | bytes 1572868
Sparse Core Ops, SparseCore 0:
  18.3 32.4 all-reduce.3
  60.0 33.1 all-reduce.5
where the time goes:
time: 195 us; the launch traced here: 194 us
  blocking collectives  78.4 us (40%)
  waiting for transfers between devices  65.8 us (34%)
  other arithmetic  17.6 us (9%)
  matrix products  16.2 us (8%)
  between operations  14.3 us (7%)
    unnamed x1, blocking collectives  49.1 us
    psum x1, waiting for transfers between devices, settle_forward(): lax.psum(partial_value.astype(jnp.bfloat16), 'tensor').astype(jnp.float32)  33.2 us
    psum x1, waiting for transfers between devices, settle_attention(): lax.psum(partial_value.astype(jnp.bfloat16), 'tensor').astype(jnp.float32)  32.6 us
    all_gather x1, blocking collectives, body(): gathered = lax.all_gather(unit_quarter, 'dp', axis=0, tiled=True)  21.9 us
    reduce_sum x1, other arithmetic, score_block(): return jnp.sum(jnp.where(chosen, tile[:, None, :], 0.0), axis=2)  10.9 us
    all_gather x1, blocking collectives, body(): scores = lax.all_gather(slice_scores, 'tensor', axis=0, tiled=True)  7.4 us
    dot_general x1, matrix products, body(): jnp.dot(activated, w_down, preferred_element_type=jnp.float32)  5.9 us
    dot_general x3, matrix products, body(): jnp.dot(hidden, w_qkv[j], preferred_element_type=jnp.float32) + b_qkv[j]  4.58 us
  transfers between devices with their start and end apart: 2, of which 2 were waited for; matrix products, arithmetic and copies ran while one was open for 0% of the time, Pallas kernels for 0%

commit v1 on v0

--- a/solution.py
+++ b/solution.py
@@ -5,6 +5,11 @@
 from jax.sharding import PartitionSpec as P
 
 HEAD = 64
+
+
+def summed_here(x, mesh_axis):
+    parts = lax.all_gather(x, mesh_axis)
+    return jnp.sum(parts, axis=0)
 
 
 def layer_norm(values, gain, shift):
@@ -21,7 +26,7 @@
 
 
 def settle_attention(partial_value, residual, bias, gain, shift):
-    total = lax.psum(partial_value.astype(jnp.bfloat16), "tensor").astype(jnp.float32)
+    total = summed_here(partial_value.astype(jnp.bfloat16), "tensor").astype(jnp.float32)
     return layer_norm(total + bias + residual.astype(jnp.float32), gain, shift).astype(jnp.bfloat16)
 
 

time: 195 us -> 184 us (0.944)
  waiting for transfers between devices: 65.8 us -> 55.2 us
    psum x1 -> x0, waiting for transfers between devices: 32.6 us -> none  [settle_attention(): lax.psum(partial_value.astype(jnp.bfloat16), 'tensor').astype(jnp.float32)]
    all_gather x0 -> x1, waiting for transfers between devices: none -> 23.3 us  [summed_here(): parts = lax.all_gather(x, mesh_axis)]
    reduce_sum x0 -> x1, other arithmetic: none -> 2.05 us  [summed_here(): return jnp.sum(parts, axis=0)]
where the time goes in v1:
time: 184 us
  blocking collectives  78.3 us (43%)
  waiting for transfers between devices  55.2 us (30%)
  other arithmetic  17.4 us (9%)
  matrix products  16.2 us (9%)
  between operations  14.3 us (8%)
  local copies, waits for them, and re-layouts  2.12 us (1%)
    unnamed x1, blocking collectives  49 us
    psum x1, waiting for transfers between devices, settle_forward(): lax.psum(partial_value.astype(jnp.bfloat16), 'tensor').astype(jnp.float32)  31.9 us
    all_gather x1, waiting for transfers between devices, summed_here(): parts = lax.all_gather(x, mesh_axis)  23.3 us
    all_gather x1, blocking collectives, body(): gathered = lax.all_gather(unit_quarter, 'dp', axis=0, tiled=True)  21.9 us
    reduce_sum x1, other arithmetic, score_block(): return jnp.sum(jnp.where(chosen, tile[:, None, :], 0.0), axis=2)  10.9 us
    all_gather x1, blocking collectives, body(): scores = lax.all_gather(slice_scores, 'tensor', axis=0, tiled=True)  7.4 us
    dot_general x1, matrix products, body(): jnp.dot(activated, w_down, preferred_element_type=jnp.float32)  5.93 us
    dot_general x3, matrix products, body(): jnp.dot(hidden, w_qkv[j], preferred_element_type=jnp.float32) + b_qkv[j]  4.59 us
  transfers between devices with their start and end apart: 2, of which 2 were waited for; matrix products, arithmetic and copies ran while one was open for 0% of the time, Pallas kernels for 0%

profile of v1, /device:TPU:15, one launch (start us, length us, event | category | flops | bytes accessed | tf_op | source)
XLA Modules:
  0.0 183.7 jit_solution(15904136766832572912)
XLA Ops:
  7.2 0.9 fusion.90
  8.1 1.6 fusion.6
  9.7 1.6 fusion.5
  11.3 0.1 copy.27
  11.4 0.1 reduce.1
  11.6 0.1 convert_reduce_fusion
  11.6 0.1 broadcast_compare_fusion
  11.8 1.3 convolution_select_fusion
  13.1 0.5 fusion.91
  13.6 1.4 fusion.4
  15.0 2.0 %convolution_convert_fusion.2 = bf16[4,64,256]{2,1,0:T(8,128)(2,1)S(1)} fusion(bf16[256,4,64]{0,2,1:T(8,128)(2,1)S(1)} %bitcast.53, f32[4,256]{1,0:T(4,128)S(1)} %fusion.91, f32[4,256,256]{1,2,0:T(8,128)} %convolution_select_fusion), kind=kOutput, calls=%fused_computation.14 | convolution fusion | flops 34407680 | bytes 1314816 | tf_op jit(solution)/shard_map/hts,shd->thd/dot_general | solution.py:72
  17.0 1.1 convolution_convert_fusion
  18.2 23.3 %all-gather.4.cloned.1.call-done = bf16[1024,1024]{1,0:T(8,128)(2,1)} async-done(((bf16[256,1024]{1,0:T(8,128)(2,1)}), bf16[1024,1024]{1,0:T(8,128)(2,1)}) %all-gather.4.cloned.1.call-update) | async-done | bytes 2097168 | tf_op jit(solution)/shard_map/all_gather | solution.py:11
  41.5 2.0 %reduce_sum.87 = bf16[256,1024]{1,0:T(8,128)(2,1)S(1)} reduce(bf16[4,256,1024]{2,1,0:T(8,128)(2,1)} %bitcast.42, bf16[]{:T(256)} %constant.49.clone.1), dimensions={0}, to_apply=%region_4.5 | reduce | flops 786432 | bytes 2621442 | tf_op jit(solution)/shard_map/reduce_sum | solution.py:12
  43.6 0.3 fusion.17
  43.9 0.3 multiply_reduce_fusion.1
  44.2 0.4 copy-done.2
  44.6 0.3 add_convert_fusion.1
  45.0 5.9 %convolution_convert_fusion.1 = bf16[256,1024]{1,0:T(8,128)(2,1)} fusion(bf16[1024,1024]{1,0:T(8,128)(2,1)S(1)} %copy-done, bf16[256,1024]{1,0:T(8,128)(2,1)S(1)} %add_convert_fusion.1, bf16[1024,1024]{1,0:T(8,128)(2,1)} %param.24, f32[1024]{0:T(1024)S(1)} %copy-done.15), kind=kOutput, calls=%fused_computation.9 | convolution fusion | flops 1091305472 | bytes 5246976 | tf_op jit(solution)/shard_map/dot_general | solution.py:79
  51.0 0.1 copy.29
  51.1 31.9 %all-reduce.3.cloned.1.call-done = bf16[256,1024]{1,0:T(8,128)(2,1)} async-done(((bf16[256,1024]{1,0:T(8,128)(2,1)}), bf16[256,1024]{1,0:T(8,128)(2,1)}) %all-reduce.3.cloned.1.call-update) | async-done | bytes 524304 | tf_op jit(solution)/shard_map/psum | solution.py:34
  83.0 1.4 fusion.18
  84.4 1.4 multiply_reduce_fusion
  85.8 0.3 add_convert_fusion
  86.2 0.3 multiply_reduce_fusion.2
  86.5 0.1 fusion.56
  86.6 21.9 %all_gather.14 = bf16[128,256]{1,0:T(8,128)(2,1)S(1)} all-gather(bf16[16,256]{1,0:T(8,128)(2,1)S(1)} %fusion.56), channel_id=1, replica_groups=mesh['dp'=8,'tensor'=4] {'dp'}, dimensions={0}, use_global_device_ids=true | all-gather | bytes 73728 | tf_op jit(solution)/shard_map/all_gather | solution.py:95
  108.5 0.5 fusion.92
  108.9 10.9 %select_reduce_fusion = f32[128,64]{1,0:T(8,128)S(1)} fusion(f32[128,2048]{1,0:T(8,128)S(1)} %fusion.92, s32[128,64]{1,0:T(8,128)S(1)} %copy.29), kind=kLoop, calls=%fused_computation.1 | loop fusion | flops 50323456 | bytes 1114112 | tf_op jit(solution)/shard_map/while/body/eval_jaxpr/reduce_sum | solution.py:110
  119.8 49.0 %all-reduce = f32[128,64]{1,0:T(8,128)S(1)} all-reduce(f32[128,64]{1,0:T(8,128)S(1)} %select_reduce_fusion), channel_id=3, replica_groups=mesh['dp'=8,'tensor'=4] {'dp','tensor'}, use_global_device_ids=true, to_apply=%region_12.13.clone | all-reduce | flops 8192 | bytes 65536
  168.9 7.4 %all-gather.1 = f32[4,4,64]{2,1,0:T(4,128)S(1)} all-gather(f32[1,4,64]{2,1,0:T(4,128)S(1)} %dynamic-slice_bitcast_fusion), channel_id=1, replica_groups=mesh['dp'=8,'tensor'=4] {'tensor'}, dimensions={0}, use_global_device_ids=true | all-gather | bytes 5120 | tf_op jit(solution)/shard_map/all_gather | solution.py:123
  176.3 0.6 copy.33
  (44 shorter events, 0.3 us)
Async XLA Ops:
  7.2 37.8 %copy-start = (bf16[1024,1024]{1,0:T(8,128)(2,1)S(1)}, bf16[1024,1024]{1,0:T(8,128)(2,1)}, u32[]{:S(2)}) copy-start(bf16[1024,1024]{1,0:T(8,128)(2,1)} %param.26) | copy-start | bytes 6291460
  7.2 4.1 %copy-start.14 = (s32[1,16]{1,0:T(1,128)S(1)}, s32[1,16]{1,0:T(1,128)}, u32[]{:S(2)}) copy-start(s32[1,16]{1,0:T(1,128)} %param.17) | copy-start | bytes 196
  7.2 34.3 %all-gather.4.cloned.1.call-start = ((), (), s32[]{:S(2)}) async-start(), calls=%async_computation.1 | async-start | bytes 2621440 | tf_op jit(solution)/shard_map/all_gather | solution.py:11
  9.7 4.0 %copy-start.1 = (bf16[256,1024]{1,0:T(8,128)(2,1)S(1)}, bf16[256,1024]{1,0:T(8,128)(2,1)}, u32[]{:S(2)}) copy-start(bf16[256,1024]{1,0:T(8,128)(2,1)} %param.16) | copy-start | bytes 1572868
  15.0 2.0 %copy-start.6 = (bf16[256,1024]{1,0:T(8,128)(2,1)S(1)}, bf16[256,1024]{1,0:T(8,128)(2,1)}, u32[]{:S(2)}) copy-start(bf16[256,1024]{1,0:T(8,128)(2,1)} %param.20) | copy-start | bytes 1572868
  17.0 26.5 %copy-start.7 = (f32[1024]{0:T(1024)S(1)}, f32[1024]{0:T(1024)}, u32[]{:S(2)}) copy-start(f32[1024]{0:T(1024)} %param.21) | copy-start | bytes 12292
  18.2 64.8 %all-reduce.3.cloned.1.call-start = ((), (), s32[]{:S(2)}) async-start(), calls=%async_computation | async-start | bytes 1048576 | tf_op jit(solution)/shard_map/psum | solution.py:34
  41.5 2.7 %copy-start.10 = (f32[1024]{0:T(1024)S(1)}, f32[1024]{0:T(1024)}, u32[]{:S(2)}) copy-start(f32[1024]{0:T(1024)} %param.23) | copy-start | bytes 12292
  41.5 2.7 %copy-start.11 = (f32[1024]{0:T(1024)S(1)}, f32[1024]{0:T(1024)}, u32[]{:S(2)}) copy-start(f32[1024]{0:T(1024)} %param.22) | copy-start | bytes 12292
  43.6 1.0 copy-start.2
  43.6 1.4 copy-start.15
  45.0 6.0 %copy-start.9 = (s32[128,64]{0,1:T(8,128)S(1)}, s32[128,64]{0,1:T(8,128)}, u32[]{:S(2)}) copy-start(s32[128,64]{0,1:T(8,128)} %param.31) | copy-start | bytes 98308
  45.0 38.0 %copy-start.8 = (f32[1024]{0:T(1024)S(1)}, f32[1024]{0:T(1024)}, u32[]{:S(2)}) copy-start(f32[1024]{0:T(1024)} %param.27) | copy-start | bytes 12292
  50.9 34.9 %copy-start.12 = (f32[1024]{0:T(1024)S(1)}, f32[1024]{0:T(1024)}, u32[]{:S(2)}) copy-start(f32[1024]{0:T(1024)} %param.29) | copy-start | bytes 12292
  50.9 34.9 %copy-start.13 = (f32[1024]{0:T(1024)S(1)}, f32[1024]{0:T(1024)}, u32[]{:S(2)}) copy-start(f32[1024]{0:T(1024)} %param.28) | copy-start | bytes 12292
  83.0 2.8 %copy-start.3 = (bf16[256,1024]{1,0:T(8,128)(2,1)S(1)}, bf16[256,1024]{1,0:T(8,128)(2,1)}, u32[]{:S(2)}) copy-start(bf16[256,1024]{1,0:T(8,128)(2,1)} %all-reduce.3.cloned.1.call-done) | copy-start | bytes 1572868
  83.0 25.4 %copy-start.5 = (bf16[2048,256]{1,0:T(8,128)(2,1)S(1)}, bf16[2048,256]{1,0:T(8,128)(2,1)}, u32[]{:S(2)}) copy-start(bf16[2048,256]{1,0:T(8,128)(2,1)} %param.30) | copy-start | bytes 3145732
  86.2 90.7 %copy-start.4 = (bf16[256,1024]{1,0:T(8,128)(2,1)}, bf16[256,1024]{1,0:T(8,128)(2,1)S(1)}, u32[]{:S(2)}) copy-start(bf16[256,1024]{1,0:T(8,128)(2,1)S(1)} %add_convert_fusion) | copy-start | bytes 1572868
Sparse Core Ops, SparseCore 0:
  18.3 23.1 all-gather.3
  51.1 31.8 all-reduce.2
